TPU v7x, 512 devices: a whole 4x8x8 slice. The times are simulated.
512 devices in a mesh: space: 32 (over y_lo, z), field: 16 (over x, y_hi, core).
Axes of the slice: x: 4, y: 8 (y_hi: 2, y_lo: 4; y = y_hi * 4 + y_lo), z: 8, core: 2. Of those that a mesh axis runs over, the one named last changes fastest.
Arguments:
- fields: float32 [16, 1024, 6144], P('field', 'space'), may hold values from -6 to 6
- zone_ids: int32 [1024, 6144], P('space'), may hold values from 0 to 7
- diffusivity: float32 [16, 8], P('field'), may hold values from 0.3 to 3
- heat_rate: float32 [15], replicated, may hold values from 0.3 to 1.5
- weight_in: bfloat16 [384, 16], replicated, may hold values from -1.5 to 1.5
- bias_in: float32 [384], replicated, may hold values from -3 to 3
- weight_mid: bfloat16 [384, 384], replicated, may hold values from -0.3125 to 0.3125
- bias_mid: float32 [384], replicated, may hold values from -3 to 3
- weight_out: bfloat16 [16, 384], replicated, may hold values from -0.3125 to 0.3125
- bias_out: float32 [16], replicated, may hold values from -2 to 2
Outputs:
- new_fields: float32 [16, 1024, 6144], P('field', 'space')
All inputs are finite; a program needn't handle non-finite values.
Results may differ from a plain program's by a relative error of at most 0.005.
Values may be sent and summed in bfloat16 or wider, within the bound.
No kernel may reach another device: no remote copies, remote signals or barrier semaphores. Data moves between devices by JAX's collectives and lax.ppermute only.
A program may use at most 64 MiB of HBM per device.

v0:
```python
import jax
import jax.numpy as jnp
from jax import lax
from jax.sharding import PartitionSpec as P

FIELDS = 16
SWEEPS = 3
ROWS_BLK = 1024
RELAX_WEIGHTS = (0.8, 1.25, 0.95)


def extended(cells, sides, width):
    for axis, dim in sides:
        count = lax.axis_size(axis)
        ends = count - 1
        head = lax.slice_in_dim(cells, 0, width, axis=dim)
        tail = lax.slice_in_dim(cells, cells.shape[dim] - width, cells.shape[dim], axis=dim)
        cells = jnp.concatenate(
            [
                lax.ppermute(tail, axis, [(i, (i + 1) % count) for i in range(ends)]),
                cells,
                lax.ppermute(head, axis, [((i + 1) % count, i) for i in range(ends)]),
            ],
            axis=dim,
        )
    return cells


def from_root(block, axis, holder):
    block = jnp.where(lax.axis_index(axis) == holder, block, jnp.zeros_like(block))
    return lax.psum(block, axis)


def relax_step(padded, source, coef_pad, weight):
    middle = padded[:, 1:-1]
    coef_mid = coef_pad[:, 1:-1]
    face_north = 0.5 * (coef_mid + coef_pad[:, 2:])
    face_south = 0.5 * (coef_mid + coef_pad[:, :-2])
    face_east = 0.5 * (coef_mid + jnp.roll(coef_mid, -1, 2))
    face_west = 0.5 * (coef_mid + jnp.roll(coef_mid, 1, 2))
    diagonal = 1.0 + face_north + face_south + face_east + face_west
    image = diagonal * middle - face_north * padded[:, 2:] - face_south * padded[:, :-2]
    image = image - face_east * jnp.roll(middle, -1, 2) - face_west * jnp.roll(middle, 1, 2)
    return middle + weight * (source - image) / diagonal


def lookup(zone_ids, diffusivity):
    coefs = jnp.zeros((diffusivity.shape[0],) + zone_ids.shape, jnp.float32)
    for number in range(diffusivity.shape[1]):
        coefs = coefs + jnp.where(
            (zone_ids == number)[None], diffusivity[:, number][:, None, None], jnp.float32(0.0)
        )
    return coefs


def on_device(
    fields,
    zone_ids,
    diffusivity,
    heat_rate,
    weight_in,
    bias_in,
    weight_mid,
    bias_mid,
    weight_out,
    bias_out,
):
    count_here, rows_here, columns = fields.shape
    coefs = lookup(zone_ids, diffusivity)
    stacked = extended(jnp.stack([fields, coefs]), (("space", 2),), 1)
    coef_pad = stacked[1]
    state = relax_step(stacked[0], fields, coef_pad, RELAX_WEIGHTS[0])
    for number in range(1, SWEEPS):
        padded = extended(state, (("space", 1),), 1)
        state = relax_step(padded, fields, coef_pad, RELAX_WEIGHTS[number])
    span = ROWS_BLK * lax.axis_size("field")
    blocks = rows_here * columns // span
    by_block = state.reshape(count_here, blocks, span)

    def one_block(row_block):
        hidden = jax.nn.silu(
            jnp.dot(weight_in, row_block, preferred_element_type=jnp.float32) + bias_in[:, None]
        ).astype(jnp.bfloat16)
        hidden = jax.nn.silu(
            jnp.dot(weight_mid, hidden, preferred_element_type=jnp.float32) + bias_mid[:, None]
        ).astype(jnp.bfloat16)
        return (
            jnp.dot(weight_out, hidden, preferred_element_type=jnp.float32) + bias_out[:, None]
        ).astype(jnp.bfloat16)

    moved = jnp.moveaxis(
        lax.all_to_all(
            by_block.astype(jnp.bfloat16), "field", split_axis=2, concat_axis=0, tiled=True
        ),
        1,
        0,
    )
    change = jnp.moveaxis(lax.map(one_block, moved), 0, 1)
    change = lax.all_to_all(change, "field", split_axis=0, concat_axis=2, tiled=True).astype(
        jnp.float32
    )
    heat_local = by_block[-1] + change[-1]
    heat_new = from_root(heat_local, "field", lax.axis_size("field") - 1)
    first_field = lax.axis_index("field") * count_here
    rate_pad = jnp.concatenate([heat_rate, jnp.zeros((1,), jnp.float32)], 0)
    rate_here = lax.dynamic_slice_in_dim(rate_pad, first_field, count_here)
    factor = jnp.exp(rate_here[:, None, None] * jnp.tanh(heat_new)[None])
    result = by_block + (change * factor).astype(jnp.bfloat16).astype(jnp.float32)
    field_ids = first_field + jnp.arange(count_here, dtype=jnp.int32)
    result = jnp.where((field_ids == FIELDS - 1)[:, None, None], heat_new[None], result)
    return result.reshape(count_here, rows_here, columns)


def solution(mesh):
    return jax.shard_map(
        on_device,
        mesh=mesh,
        in_specs=(
            P("field", "space", None),
            P("space", None),
            P("field", None),
            P(),
            P(),
            P(),
            P(),
            P(),
            P(),
            P(),
        ),
        out_specs=P("field", "space", None),
        check_vma=False,
    )
```

profile of v0, /device:TPU:1, one launch (start us, length us, event | category | flops | bytes accessed | tf_op | source)
XLA Modules:
  0.0 460.7 jit_solution(11899596553922637642)
XLA Ops:
  6.5 1.6 fusion.65
  8.2 6.7 %add_bitcast_fusion = f32[1,1,32,6144]{3,2,1,0:T(8,128)S(1)} fusion(s32[32,6144]{1,0:T(8,128)} %param.13, f32[]{:T(128)} %bitcast.13, f32[]{:T(128)} %bitcast.12, f32[]{:T(128)} %bitcast.11, f32[]{:T(128)} %bitcast.10, f32[]{:T(128)} %bitcast.9, f32[]{:T(128)} %bitcast.8, f32[]{:T(128)} %bitcast.7, f32[]{:T(128)} %bitcast.6), kind=kLoop, calls=%fused_computation.80 | loop fusion | flops 4521984 | bytes 1572896 | tf_op jit(solution)/shard_map/stack | solution.py:70
  14.9 4.8 %collective-permute-start = (f32[2,1,1,6144]{3,2,1,0:T(1,128)S(1)}, f32[2,1,1,6144]{3,2,1,0:T(1,128)S(1)}, u32[]{:S(2)}, u32[]{:S(2)}) collective-permute-start(f32[2,1,1,6144]{3,2,1,0:T(1,128)S(1)} %get-tuple-element.78), channel_id=1, source_target_pairs={{0,16},{16,32},{32,48},{48,64},{64,80},{80,96},{96,112},{112,128},... | collective-permute-start | bytes 147464 | tf_op jit(solution)/shard_map/ppermute | solution.py:20
  19.8 1.3 collective-permute-start.1
  21.1 4.2 collective-permute-done.1
  25.6 0.5 fusion.55
  26.3 1.0 fusion.45
  27.3 0.3 fusion.63
  27.6 1.3 collective-permute-start.2
  28.9 4.6 %collective-permute-start.3 = (f32[1,1,6144]{2,1,0:T(1,128)S(1)}, f32[1,1,6144]{2,1,0:T(1,128)S(1)}, u32[]{:S(2)}, u32[]{:S(2)}) collective-permute-start(f32[1,1,6144]{2,1,0:T(1,128)S(1)} %get-tuple-element.99), channel_id=1, source_target_pairs={{0,16},{16,32},{32,48},{48,64},{64,80},{80,96},{96,112},{112,128},... | collective-permute-start | bytes 73736 | tf_op jit(solution)/shard_map/ppermute | solution.py:20
  33.6 0.9 collective-permute-done.3
  34.4 0.9 fusion.36
  35.3 0.3 fusion.60
  35.6 1.3 collective-permute-start.4
  36.9 6.0 %collective-permute-start.5 = (f32[1,1,6144]{2,1,0:T(1,128)S(1)}, f32[1,1,6144]{2,1,0:T(1,128)S(1)}, u32[]{:S(2)}, u32[]{:S(2)}) collective-permute-start(f32[1,1,6144]{2,1,0:T(1,128)S(1)} %get-tuple-element.89), channel_id=1, source_target_pairs={{0,16},{16,32},{32,48},{48,64},{64,80},{80,96},{96,112},{112,128},... | collective-permute-start | bytes 73736 | tf_op jit(solution)/shard_map/ppermute | solution.py:20
  43.0 0.7 collective-permute-done.5
  43.7 0.9 fusion.51
  44.6 0.6 convert_element_type.50
  45.2 12.8 %copy.13 = bf16[1,12,16384]{1,0,2:T(2,128)(2,1)} copy(bf16[1,12,16384]{2,1,0:T(8,128)(2,1)S(1)} %convert_element_type.50) | data formatting | bytes 786432 | tf_op jit(solution)/shard_map/convert_element_type | solution.py:93
  58.0 0.5 broadcast.69
  58.5 90.8 %reduce = bf16[16384,12]{1,0:T(8,128)(2,1)} reduce(bf16[16384,1,12]{2,1,0:T(2,128)(2,1)} %bitcast.109, bf16[]{:T(256)} %broadcast.69), dimensions={1}, to_apply=%bitcast.85.reduce_sub_computation | reduce | bytes 786434
  149.3 9.5 %reshape.89 = bf16[16,2,6144]{2,1,0:T(2,128)(2,1)} reshape(bf16[16384,12]{1,0:T(8,128)(2,1)} %reduce) | data formatting | bytes 786432
  158.9 13.1 %all-to-all-start = ((bf16[16,2,6144]{2,1,0:T(2,128)(2,1)}), bf16[16,2,6144]{2,1,0:T(2,128)(2,1)S(1)}, u32[]{:S(2)}, u32[]{:S(2)}) async-start(bf16[16,2,6144]{2,1,0:T(2,128)(2,1)} %reshape.89), calls=%async_computation | async-start | bytes 786432 | tf_op jit(solution)/shard_map/all_to_all | solution.py:92
  172.0 12.3 %all-to-all-done = bf16[16,2,6144]{2,1,0:T(2,128)(2,1)S(1)} async-done(((bf16[16,2,6144]{2,1,0:T(2,128)(2,1)}), bf16[16,2,6144]{2,1,0:T(2,128)(2,1)S(1)}, u32[]{:S(2)}, u32[]{:S(2)}) %all-to-all-start) | async-done | bytes 393248 | tf_op jit(solution)/shard_map/all_to_all | solution.py:92
  184.3 12.2 %reshape.90 = bf16[16384,1,12]{2,1,0:T(2,128)(2,1)} reshape(bf16[16,2,6144]{2,1,0:T(2,128)(2,1)S(1)} %all-to-all-done) | data formatting | bytes 786432
  196.5 15.4 %copy.14 = bf16[1,12,16384]{2,1,0:T(8,128)(2,1)S(1)} copy(bf16[1,12,16384]{1,0,2:T(2,128)(2,1)} %bitcast.110) | data formatting | bytes 786432 | tf_op jit(solution)/shard_map/all_to_all | solution.py:92
  212.0 0.3 copy.17
  212.3 0.6 copy-done.1
  212.9 19.7 %while.10 = (s32[]{:T(128)}, bf16[12,16,1024]{2,1,0:T(8,128)(2,1)S(1)}, bf16[12,16,1024]{2,1,0:T(8,128)(2,1)S(1)}, bf16[384,16]{0,1:T(8,128)(2,1)S(1)}, f32[384]...) while((s32[]{:T(128)}, ...), condition=%wide.region_1.2_spmd, body=%wide.region_0.1_spmd.sunk | while | flops 331907072 | bytes 1962605 | solution.py:98
  212.9 0.6 fusion.82
  213.5 1.0 fusion.83
  214.5 0.6 fusion.82
  215.1 1.0 fusion.83
  216.1 0.6 fusion.82
  216.8 1.0 fusion.83
  217.8 0.6 fusion.82
  218.4 1.0 fusion.83
  219.4 0.6 fusion.82
  220.1 1.0 fusion.83
  221.1 0.6 fusion.82
  221.7 1.0 fusion.83
  222.7 0.6 fusion.82
  223.4 1.0 fusion.83
  224.4 0.6 fusion.82
  225.0 1.0 fusion.83
  226.0 0.6 fusion.82
  226.6 1.0 fusion.83
  227.6 0.6 fusion.82
  228.3 1.0 fusion.83
  229.3 0.6 fusion.82
  229.9 1.0 fusion.83
  230.9 0.6 fusion.82
  231.6 1.0 fusion.83
  232.6 1.1 copy.22
  233.6 4.5 all-to-all-start.1
  238.2 0.3 squeeze_reshape.3
  238.5 13.4 %all-to-all-done.1 = bf16[16,12,1024]{2,1,0:T(8,128)(2,1)S(1)} async-done(((bf16[16,12,1024]{2,1,0:T(8,128)(2,1)}), bf16[16,12,1024]{2,1,0:T(8,128)(2,1)S(1)}, u32[]{:S(2)}, u32[]{:S(2)}) %all-to-all-start.1) | async-done | bytes 393248 | tf_op jit(solution)/shard_map/all_to_all | solution.py:99
  252.0 0.5 copy.21
  252.6 0.6 copy.18
  253.3 1.1 add_select_fusion.1
  254.4 0.6 dynamic_slice.7
  255.0 195.6 %all-reduce.2.cloned.1.call-done = f32[12,16384]{1,0:T(8,128)} async-done(((f32[12,16384]{1,0:T(8,128)}), f32[12,16384]{1,0:T(8,128)}) %all-reduce.2.cloned.1.call-update) | async-done | bytes 786448 | tf_op jit(solution)/shard_map/psum | solution.py:31
  450.6 2.2 add_select_fusion
  452.7 1.1 reshape.86
  (33 shorter events, 1.2 us)
Async XLA Ops:
  6.5 8.3 %copy-start = (f32[1,32,6144]{2,1,0:T(8,128)S(1)}, f32[1,32,6144]{2,1,0:T(8,128)}, u32[]{:S(2)}) copy-start(f32[1,32,6144]{2,1,0:T(8,128)} %param.12) | copy-start | bytes 2359300
  14.9 6.1 %collective-permute-start = (f32[2,1,1,6144]{3,2,1,0:T(1,128)S(1)}, f32[2,1,1,6144]{3,2,1,0:T(1,128)S(1)}, u32[]{:S(2)}, u32[]{:S(2)}) collective-permute-start(f32[2,1,1,6144]{3,2,1,0:T(1,128)S(1)} %get-tuple-element.78), channel_id=1, source_target_pairs={{0,16},{16,32},{32,48},{48,64},{64,80},{80,96},{96,112},{112,128},... | collective-permute-start | bytes 147464 | tf_op jit(solution)/shard_map/ppermute | solution.py:20
  19.8 5.5 %collective-permute-start.1 = (f32[2,1,1,6144]{3,2,1,0:T(1,128)S(1)}, f32[2,1,1,6144]{3,2,1,0:T(1,128)S(1)}, u32[]{:S(2)}, u32[]{:S(2)}) collective-permute-start(f32[2,1,1,6144]{3,2,1,0:T(1,128)S(1)} %get-tuple-element.79), channel_id=1, source_target_pairs={{16,0},{32,16},{48,32},{64,48},{80,64},{96,80},{112,96},{128,112},... | collective-permute-start | bytes 147464 | tf_op jit(solution)/shard_map/ppermute | solution.py:22
  27.6 6.0 %collective-permute-start.2 = (f32[1,1,6144]{2,1,0:T(1,128)S(1)}, f32[1,1,6144]{2,1,0:T(1,128)S(1)}, u32[]{:S(2)}, u32[]{:S(2)}) collective-permute-start(f32[1,1,6144]{2,1,0:T(1,128)S(1)} %get-tuple-element.98), channel_id=1, source_target_pairs={{16,0},{32,16},{48,32},{64,48},{80,64},{96,80},{112,96},{128,112},... | collective-permute-start | bytes 73736 | tf_op jit(solution)/shard_map/ppermute | solution.py:22
  28.9 5.6 %collective-permute-start.3 = (f32[1,1,6144]{2,1,0:T(1,128)S(1)}, f32[1,1,6144]{2,1,0:T(1,128)S(1)}, u32[]{:S(2)}, u32[]{:S(2)}) collective-permute-start(f32[1,1,6144]{2,1,0:T(1,128)S(1)} %get-tuple-element.99), channel_id=1, source_target_pairs={{0,16},{16,32},{32,48},{48,64},{64,80},{80,96},{96,112},{112,128},... | collective-permute-start | bytes 73736 | tf_op jit(solution)/shard_map/ppermute | solution.py:20
  35.6 7.4 %collective-permute-start.4 = (f32[1,1,6144]{2,1,0:T(1,128)S(1)}, f32[1,1,6144]{2,1,0:T(1,128)S(1)}, u32[]{:S(2)}, u32[]{:S(2)}) collective-permute-start(f32[1,1,6144]{2,1,0:T(1,128)S(1)} %get-tuple-element.88), channel_id=1, source_target_pairs={{16,0},{32,16},{48,32},{64,48},{80,64},{96,80},{112,96},{128,112},... | collective-permute-start | bytes 73736 | tf_op jit(solution)/shard_map/ppermute | solution.py:22
  36.9 6.8 %collective-permute-start.5 = (f32[1,1,6144]{2,1,0:T(1,128)S(1)}, f32[1,1,6144]{2,1,0:T(1,128)S(1)}, u32[]{:S(2)}, u32[]{:S(2)}) collective-permute-start(f32[1,1,6144]{2,1,0:T(1,128)S(1)} %get-tuple-element.89), channel_id=1, source_target_pairs={{0,16},{16,32},{32,48},{48,64},{64,80},{80,96},{96,112},{112,128},... | collective-permute-start | bytes 73736 | tf_op jit(solution)/shard_map/ppermute | solution.py:20
  158.9 25.4 %all-to-all-start = ((bf16[16,2,6144]{2,1,0:T(2,128)(2,1)}), bf16[16,2,6144]{2,1,0:T(2,128)(2,1)S(1)}, u32[]{:S(2)}, u32[]{:S(2)}) async-start(bf16[16,2,6144]{2,1,0:T(2,128)(2,1)} %reshape.89), calls=%async_computation | async-start | bytes 786432 | tf_op jit(solution)/shard_map/all_to_all | solution.py:92
  211.9 1.0 copy-start.1
  211.9 1.0 copy-start.2
  211.9 0.9 copy-start.3
  211.9 0.9 copy-start.4
  211.9 0.9 copy-start.5
  212.0 0.9 copy-start.6
  233.6 18.3 %all-to-all-start.1 = ((bf16[16,12,1024]{2,1,0:T(8,128)(2,1)}), bf16[16,12,1024]{2,1,0:T(8,128)(2,1)S(1)}, u32[]{:S(2)}, u32[]{:S(2)}) async-start(bf16[16,12,1024]{2,1,0:T(8,128)(2,1)} %bitcast.92), calls=%async_computation.1 | async-start | bytes 1048576 | tf_op jit(solution)/shard_map/all_to_all | solution.py:99
  238.2 212.4 %all-reduce.2.cloned.1.call-start = ((), (), s32[]{:S(2)}) async-start(), calls=%async_computation.2 | async-start | bytes 2097152 | tf_op jit(solution)/shard_map/psum | solution.py:31
  253.2 1.1 copy-start.7
Sparse Core Ops, SparseCore 0:
  254.5 196.0 all-reduce.1
where the time goes:
time: 462 us; the launch traced here: 461 us
  waiting for transfers between devices  227 us (49%)
  other arithmetic  104 us (23%)
  local copies, waits for them, and re-layouts  59.4 us (13%)
  starting transfers between devices  37 us (8%)
  matrix products  19.6 us (4%)
  between operations  13.7 us (3%)
    psum x1, waiting for transfers between devices, from_root(): return lax.psum(block, axis)  196 us
    unnamed x1, other arithmetic  90.8 us
    unnamed x22, local copies, waits for them, and re-layouts  23.9 us
    ppermute x3, starting transfers between devices, extended(): lax.ppermute(tail, axis, [(i, (i + 1) % count) for i in range(ends)])  15.5 us
    all_to_all x1, local copies, waits for them, and re-layouts, on_device(): lax.all_to_all(by_block.astype(jnp.bfloat16), 'field', split_axis=2, conc...  15.4 us
    all_to_all x1, waiting for transfers between devices, on_device(): lax.all_to_all(change, 'field', split_axis=0, concat_axis=2, tiled=True)  13.4 us
    convert_element_type x2, local copies, waits for them, and re-layouts, on_device(): by_block.astype(jnp.bfloat16)  13.4 us
    all_to_all x1, starting transfers between devices, on_device(): lax.all_to_all(by_block.astype(jnp.bfloat16), 'field', split_axis=2, conc...  13.1 us
  transfers between devices with their start and end apart: 9, of which 6 were waited for; matrix products, arithmetic and copies ran while one was open for 0% of the time, Pallas kernels for 0%

commit v1 on v0

--- a/solution.py
+++ b/solution.py
@@ -7,6 +7,7 @@
 SWEEPS = 3
 ROWS_BLK = 1024
 RELAX_WEIGHTS = (0.8, 1.25, 0.95)
+modes_note = lambda mine, link_axis: lax.all_gather(mine, link_axis).sum(axis=0)
 
 
 def extended(cells, sides, width):
@@ -28,7 +29,7 @@
 
 def from_root(block, axis, holder):
     block = jnp.where(lax.axis_index(axis) == holder, block, jnp.zeros_like(block))
-    return lax.psum(block, axis)
+    return modes_note(block, axis)
 
 
 def relax_step(padded, source, coef_pad, weight):

time: 462 us -> 489 us (1.058)
  matrix products: 19.6 us -> 43.5 us
  waiting for transfers between devices: 227 us -> 216 us
  other arithmetic: 104 us -> 113 us
    psum x1 -> x0, waiting for transfers between devices: 196 us -> none  [from_root(): return lax.psum(block, axis)]
    all_gather x0 -> x1, waiting for transfers between devices: none -> 184 us  [lax.all_gather(mine, link_axis).sum(axis=0)]
    dot_general x12, matrix products: 12 us -> 25.4 us  [one_block(): jnp.dot(weight_out, hidden, preferred_element_type=jnp.float32)]
    dot_general x12, matrix products: 7.58 us -> 18.2 us  [one_block(): jnp.dot(weight_in, row_block, preferred_element_type=jnp.float32)]
    reduce_sum x0 -> x1, other arithmetic: none -> 6.86 us  [lax.all_gather(mine, link_axis).sum(axis=0)]
    convert_element_type x1 -> x4, local copies, waits for them, and re-layouts: 0.46 us -> 5.42 us  [on_device(): lax.all_to_all(change, 'field', split_axis=0, concat_axis=2, tiled=True)]
    unnamed x22 -> x18, local copies, waits for them, and re-layouts: 23.9 us -> 22.9 us
    convert_element_type x2 -> x1, local copies, waits for them, and re-layouts: 13.4 us -> 12.9 us  [on_device(): by_block.astype(jnp.bfloat16)]
  transfers between devices with their start and end apart: 9 -> 9, of which waited for: 6 -> 6; matrix products, arithmetic and copies ran while one was open for 0% -> 1% of each run, Pallas kernels for 0% -> 0%
where the time goes in v1:
time: 489 us; the launch traced here: 485 us
  waiting for transfers between devices  216 us (44%)
  other arithmetic  113 us (23%)
  local copies, waits for them, and re-layouts  62.1 us (13%)
  matrix products  43.5 us (9%)
  starting transfers between devices  37.2 us (8%)
  between operations  13.6 us (3%)
    all_gather x1, waiting for transfers between devices, lax.all_gather(mine, link_axis).sum(axis=0)  184 us
    unnamed x1, other arithmetic  90.8 us
    dot_general x12, matrix products, one_block(): jnp.dot(weight_out, hidden, preferred_element_type=jnp.float32)  25.4 us
    unnamed x18, local copies, waits for them, and re-layouts  22.9 us
    dot_general x12, matrix products, one_block(): jnp.dot(weight_in, row_block, preferred_element_type=jnp.float32)  18.2 us
    ppermute x3, starting transfers between devices, extended(): lax.ppermute(tail, axis, [(i, (i + 1) % count) for i in range(ends)])  15.5 us
    all_to_all x1, local copies, waits for them, and re-layouts, on_device(): lax.all_to_all(by_block.astype(jnp.bfloat16), 'field', split_axis=2, conc...  15.4 us
    all_to_all x1, waiting for transfers between devices, on_device(): lax.all_to_all(change, 'field', split_axis=0, concat_axis=2, tiled=True)  13.7 us
  transfers between devices with their start and end apart: 9, of which 6 were waited for; matrix products, arithmetic and copies ran while one was open for 1% of the time, Pallas kernels for 0%

profile of v1, /device:TPU:1, one launch (start us, length us, event | category | flops | bytes accessed | tf_op | source)
XLA Modules:
  0.0 485.4 jit_solution(2256536463914739264)
XLA Ops:
  6.5 1.6 fusion.63
  8.2 6.8 %add_bitcast_fusion = f32[1,1,32,6144]{3,2,1,0:T(8,128)S(1)} fusion(s32[32,6144]{1,0:T(8,128)} %param.13, f32[]{:T(128)} %bitcast.13, f32[]{:T(128)} %bitcast.12, f32[]{:T(128)} %bitcast.11, f32[]{:T(128)} %bitcast.10, f32[]{:T(128)} %bitcast.9, f32[]{:T(128)} %bitcast.8, f32[]{:T(128)} %bitcast.7, f32[]{:T(128)} %bitcast.6), kind=kLoop, calls=%fused_computation.79 | loop fusion | flops 4521984 | bytes 1572896 | tf_op jit(solution)/shard_map/stack | solution.py:71
  15.1 4.8 collective-permute-start
  19.9 1.3 collective-permute-start.1
  21.2 4.2 collective-permute-done.1
  25.8 0.5 fusion.53
  26.4 1.0 fusion.45
  27.7 1.3 collective-permute-start.2
  29.0 4.6 collective-permute-start.3
  33.7 0.9 collective-permute-done.3
  34.6 0.9 fusion.36
  35.5 0.3 fusion.58
  35.8 1.3 collective-permute-start.4
  37.1 6.0 %collective-permute-start.5 = (f32[1,1,6144]{2,1,0:T(1,128)S(1)}, f32[1,1,6144]{2,1,0:T(1,128)S(1)}, u32[]{:S(2)}, u32[]{:S(2)}) collective-permute-start(f32[1,1,6144]{2,1,0:T(1,128)S(1)} %get-tuple-element.91), channel_id=1, source_target_pairs={{0,16},{16,32},{32,48},{48,64},{64,80},{80,96},{96,112},{112,128},... | collective-permute-start | bytes 73736 | tf_op jit(solution)/shard_map/ppermute | solution.py:21
  43.2 0.7 collective-permute-done.5
  43.9 0.9 fusion.26
  44.7 0.3 squeeze_reshape.3
  45.1 12.9 %copy.17 = bf16[1,12,16384]{1,0,2:T(2,128)(2,1)} copy(bf16[1,12,16384]{2,1,0:T(8,128)(2,1)S(1)} %convert_element_type.84) | data formatting | bytes 786432 | tf_op jit(solution)/shard_map/convert_element_type | solution.py:94
  58.0 0.5 broadcast.91
  58.5 90.8 %reduce = bf16[16384,12]{1,0:T(8,128)(2,1)} reduce(bf16[16384,1,12]{2,1,0:T(2,128)(2,1)} %bitcast.109, bf16[]{:T(256)} %broadcast.91), dimensions={1}, to_apply=%bitcast.86.reduce_sub_computation | reduce | bytes 786434
  149.3 9.5 %reshape.152 = bf16[16,2,6144]{2,1,0:T(2,128)(2,1)} reshape(bf16[16384,12]{1,0:T(8,128)(2,1)} %reduce) | data formatting | bytes 786432
  158.8 13.1 %all-to-all-start = ((bf16[16,2,6144]{2,1,0:T(2,128)(2,1)}), bf16[16,2,6144]{2,1,0:T(2,128)(2,1)S(1)}, u32[]{:S(2)}, u32[]{:S(2)}) async-start(bf16[16,2,6144]{2,1,0:T(2,128)(2,1)} %reshape.152), calls=%async_computation | async-start | bytes 786432 | tf_op jit(solution)/shard_map/all_to_all | solution.py:93
  171.9 12.3 %all-to-all-done = bf16[16,2,6144]{2,1,0:T(2,128)(2,1)S(1)} async-done(((bf16[16,2,6144]{2,1,0:T(2,128)(2,1)}), bf16[16,2,6144]{2,1,0:T(2,128)(2,1)S(1)}, u32[]{:S(2)}, u32[]{:S(2)}) %all-to-all-start) | async-done | bytes 393248 | tf_op jit(solution)/shard_map/all_to_all | solution.py:93
  184.2 12.2 %reshape.153 = bf16[16384,1,12]{2,1,0:T(2,128)(2,1)} reshape(bf16[16,2,6144]{2,1,0:T(2,128)(2,1)S(1)} %all-to-all-done) | data formatting | bytes 786432
  196.4 15.4 %copy.18 = bf16[1,12,16384]{2,1,0:T(8,128)(2,1)S(1)} copy(bf16[1,12,16384]{1,0,2:T(2,128)(2,1)} %bitcast.110) | data formatting | bytes 786432 | tf_op jit(solution)/shard_map/all_to_all | solution.py:93
  211.9 0.3 copy.23
  212.2 0.3 copy-done.2
  212.6 43.6 %while.10 = (s32[]{:T(128)}, bf16[12,16,1024]{2,1,0:T(8,128)(2,1)S(1)}, bf16[12,16,1024]{2,1,0:T(8,128)(2,1)S(1)}, bf16[384,16]{0,1:T(8,128)(2,1)S(1)}, f32[384]...) while((s32[]{:T(128)}, ...), condition=%wide.region_1.2_spmd, body=%wide.region_0.1_spmd.sunk | while | flops 331907072 | bytes 3142289 | solution.py:99
  212.6 1.5 fusion.80
  214.1 2.1 fusion.81
  216.2 1.5 fusion.80
  217.7 2.1 fusion.81
  219.8 1.5 fusion.80
  221.4 2.1 fusion.81
  223.5 1.5 fusion.80
  225.0 2.1 fusion.81
  227.1 1.5 fusion.80
  228.6 2.1 fusion.81
  230.8 1.5 fusion.80
  232.3 2.1 fusion.81
  234.4 1.5 fusion.80
  235.9 2.1 fusion.81
  238.0 1.5 fusion.80
  239.6 2.1 fusion.81
  241.7 1.5 fusion.80
  243.2 2.1 fusion.81
  245.3 1.5 fusion.80
  246.8 2.1 fusion.81
  248.9 1.5 fusion.80
  250.5 2.1 fusion.81
  252.6 1.5 fusion.80
  254.1 2.1 fusion.81
  256.2 1.1 copy.25
  257.3 4.8 all-to-all-start.1
  262.1 13.7 %all-to-all-done.1 = bf16[16,12,1024]{2,1,0:T(8,128)(2,1)S(1)} async-done(((bf16[16,12,1024]{2,1,0:T(8,128)(2,1)}), bf16[16,12,1024]{2,1,0:T(8,128)(2,1)S(1)}, u32[]{:S(2)}, u32[]{:S(2)}) %all-to-all-start.1) | async-done | bytes 393248 | tf_op jit(solution)/shard_map/all_to_all | solution.py:100
  275.9 1.3 copy.20
  277.3 2.4 reshape.151
  279.7 2.3 add_select_fusion
  282.1 0.7 dynamic_slice.7
  282.8 0.5 copy.22
  283.2 1.2 reshape.148
  284.5 184.1 %all-gather.2.cloned.1.call-done = f32[16,12,16384]{2,1,0:T(8,128)} async-done(((f32[1,12,16384]{2,1,0:T(8,128)}), f32[16,12,16384]{2,1,0:T(8,128)}) %all-gather.2.cloned.1.call-update) | async-done | bytes 12582928 | tf_op jit(solution)/shard_map/all_gather | solution.py:10
  468.6 6.9 %reduce_sum.11 = f32[12,16384]{1,0:T(8,128)S(1)} reduce(f32[16,12,16384]{2,1,0:T(8,128)} %all-gather.2.cloned.1.call-done, f32[]{:T(128)} %constant.8.clone.1), dimensions={0}, to_apply=%region_2.3 | reduce | flops 2949120 | bytes 13369348 | tf_op jit(solution)/shard_map/reduce_sum | solution.py:10
  475.7 2.9 add_select_fusion.1
  (57 shorter events, 1.7 us)
Async XLA Ops:
  6.5 8.4 %copy-start = (f32[1,32,6144]{2,1,0:T(8,128)S(1)}, f32[1,32,6144]{2,1,0:T(8,128)}, u32[]{:S(2)}) copy-start(f32[1,32,6144]{2,1,0:T(8,128)} %param.12) | copy-start | bytes 2359300
  15.1 6.1 %collective-permute-start = (f32[2,1,1,6144]{3,2,1,0:T(1,128)S(1)}, f32[2,1,1,6144]{3,2,1,0:T(1,128)S(1)}, u32[]{:S(2)}, u32[]{:S(2)}) collective-permute-start(f32[2,1,1,6144]{3,2,1,0:T(1,128)S(1)} %get-tuple-element.76), channel_id=1, source_target_pairs={{0,16},{16,32},{32,48},{48,64},{64,80},{80,96},{96,112},{112,128},... | collective-permute-start | bytes 147464 | tf_op jit(solution)/shard_map/ppermute | solution.py:21
  19.9 5.5 %collective-permute-start.1 = (f32[2,1,1,6144]{3,2,1,0:T(1,128)S(1)}, f32[2,1,1,6144]{3,2,1,0:T(1,128)S(1)}, u32[]{:S(2)}, u32[]{:S(2)}) collective-permute-start(f32[2,1,1,6144]{3,2,1,0:T(1,128)S(1)} %get-tuple-element.77), channel_id=1, source_target_pairs={{16,0},{32,16},{48,32},{64,48},{80,64},{96,80},{112,96},{128,112},... | collective-permute-start | bytes 147464 | tf_op jit(solution)/shard_map/ppermute | solution.py:23
  27.7 6.0 %collective-permute-start.2 = (f32[1,1,6144]{2,1,0:T(1,128)S(1)}, f32[1,1,6144]{2,1,0:T(1,128)S(1)}, u32[]{:S(2)}, u32[]{:S(2)}) collective-permute-start(f32[1,1,6144]{2,1,0:T(1,128)S(1)} %get-tuple-element.96), channel_id=1, source_target_pairs={{16,0},{32,16},{48,32},{64,48},{80,64},{96,80},{112,96},{128,112},... | collective-permute-start | bytes 73736 | tf_op jit(solution)/shard_map/ppermute | solution.py:23
  29.0 5.6 %collective-permute-start.3 = (f32[1,1,6144]{2,1,0:T(1,128)S(1)}, f32[1,1,6144]{2,1,0:T(1,128)S(1)}, u32[]{:S(2)}, u32[]{:S(2)}) collective-permute-start(f32[1,1,6144]{2,1,0:T(1,128)S(1)} %get-tuple-element.97), channel_id=1, source_target_pairs={{0,16},{16,32},{32,48},{48,64},{64,80},{80,96},{96,112},{112,128},... | collective-permute-start | bytes 73736 | tf_op jit(solution)/shard_map/ppermute | solution.py:21
  35.8 7.4 %collective-permute-start.4 = (f32[1,1,6144]{2,1,0:T(1,128)S(1)}, f32[1,1,6144]{2,1,0:T(1,128)S(1)}, u32[]{:S(2)}, u32[]{:S(2)}) collective-permute-start(f32[1,1,6144]{2,1,0:T(1,128)S(1)} %get-tuple-element.90), channel_id=1, source_target_pairs={{16,0},{32,16},{48,32},{64,48},{80,64},{96,80},{112,96},{128,112},... | collective-permute-start | bytes 73736 | tf_op jit(solution)/shard_map/ppermute | solution.py:23
  37.1 6.8 %collective-permute-start.5 = (f32[1,1,6144]{2,1,0:T(1,128)S(1)}, f32[1,1,6144]{2,1,0:T(1,128)S(1)}, u32[]{:S(2)}, u32[]{:S(2)}) collective-permute-start(f32[1,1,6144]{2,1,0:T(1,128)S(1)} %get-tuple-element.91), channel_id=1, source_target_pairs={{0,16},{16,32},{32,48},{48,64},{64,80},{80,96},{96,112},{112,128},... | collective-permute-start | bytes 73736 | tf_op jit(solution)/shard_map/ppermute | solution.py:21
  158.8 25.4 %all-to-all-start = ((bf16[16,2,6144]{2,1,0:T(2,128)(2,1)}), bf16[16,2,6144]{2,1,0:T(2,128)(2,1)S(1)}, u32[]{:S(2)}, u32[]{:S(2)}) async-start(bf16[16,2,6144]{2,1,0:T(2,128)(2,1)} %reshape.152), calls=%async_computation | async-start | bytes 786432 | tf_op jit(solution)/shard_map/all_to_all | solution.py:93
  211.9 0.7 copy-start.2
  211.9 0.7 copy-start.3
  211.9 0.7 copy-start.4
  211.9 0.7 copy-start.5
  211.9 0.7 copy-start.6
  212.6 1.5 copy-start.1
  216.2 1.5 copy-start.1
  219.8 1.5 copy-start.1
  223.5 1.5 copy-start.1
  227.1 1.5 copy-start.1
  230.8 1.5 copy-start.1
  234.4 1.5 copy-start.1
  238.0 1.5 copy-start.1
  241.7 1.5 copy-start.1
  245.3 1.5 copy-start.1
  248.9 1.5 copy-start.1
  252.6 1.5 copy-start.1
  257.3 18.5 %all-to-all-start.1 = ((bf16[16,12,1024]{2,1,0:T(8,128)(2,1)}), bf16[16,12,1024]{2,1,0:T(8,128)(2,1)S(1)}, u32[]{:S(2)}, u32[]{:S(2)}) async-start(bf16[16,12,1024]{2,1,0:T(8,128)(2,1)} %bitcast.92), calls=%async_computation.1 | async-start | bytes 1048576 | tf_op jit(solution)/shard_map/all_to_all | solution.py:100
  262.0 206.6 %all-gather.2.cloned.1.call-start = ((), (), s32[]{:S(2)}) async-start(), calls=%async_computation.2 | async-start | bytes 17825792 | tf_op jit(solution)/shard_map/all_gather | solution.py:10
  279.7 2.4 copy-start.7
Sparse Core Ops, SparseCore 0:
  282.2 186.4 all-gather.1
